TPU v7x, 512 devices: a whole 4x4x16 slice. The times are simulated.
512 devices in a mesh: seq: 128 (over y, z, core), head: 4 (over x).
Axes of the slice: x: 4, y: 4, z: 16, core: 2. Of those that a mesh axis runs over, the one named last changes fastest.
Arguments:
- tokens: bfloat16 [64, 4, 1024], P('head'), may hold values from -6 to 6
- cache_keys: bfloat16 [64, 4096, 512], P(None, 'seq', 'head'), may hold values from -70 to 70
- cache_values: bfloat16 [64, 4096, 512], P(None, 'seq', 'head'), may hold values from -6 to 6
- held_states: bfloat16 [64, 512, 1024], P(None, 'seq'), may hold values from -6 to 6
- recompute_pos: int32 [64, 512], P(None, 'seq'), may hold values from 0 to 4095, as said below
- cache_len: int32 [64], replicated, may hold values from 1 to 4096
- new_prompt: int32 [64], replicated, may hold values 0 or 1
- w_qkv: bfloat16 [3, 1024, 512], P(None, None, 'head'), may hold values from -0.1875 to 0.1875
- qkv_bias: float32 [3, 512], P(None, 'head'), may hold values from -3 to 3
- w_out: bfloat16 [512, 1024], P('head'), may hold values from -1.5 to 1.5
- out_bias: float32 [1024], replicated, may hold values from -3 to 3
- attn_gain: float32 [1024], replicated, may hold values from 0.1 to 1.9
- attn_shift: float32 [1024], replicated, may hold values from -3 to 3
- w_up: bfloat16 [1024, 2048], P(None, 'head'), may hold values from -0.1875 to 0.1875
- up_bias: float32 [2048], P('head'), may hold values from -3 to 3
- w_down: bfloat16 [2048, 1024], P('head'), may hold values from -0.125 to 0.125
- down_bias: float32 [1024], replicated, may hold values from -3 to 3
- ffn_gain: float32 [1024], replicated, may hold values from 0.1 to 1.9
- ffn_shift: float32 [1024], replicated, may hold values from -3 to 3
Outputs:
- layer_out: bfloat16 [64, 4, 1024], P('head')
Inputs may be any that keep to these rules, and one draw needn't show every extreme that they name: `recompute_pos`: columns s * 4 to (s + 1) * 4 - 1 of a row hold distinct positions from s * 32 to (s + 1) * 32 - 1.
All inputs are finite; a program needn't handle non-finite values.
Results may differ from a plain program's by a relative error of at most 0.011.
Values may be sent and summed in bfloat16 or wider, within the bound.
No kernel may reach another device: no remote copies, remote signals or barrier semaphores. Data moves between devices by JAX's collectives and lax.ppermute only.
A program may use at most 192 MiB of HBM per device.

v0:
```python
import jax
import jax.numpy as jnp
from jax import lax
from jax.sharding import PartitionSpec as P

HDIM = 64
NEG = -1e30
EPS = 1e-05


def layer_norm(values, norm_gain, norm_bias):
    center = jnp.mean(values, axis=-1, keepdims=True)
    spread = values - center
    second = jnp.mean(spread * spread, axis=-1, keepdims=True)
    return spread * lax.rsqrt(second + EPS) * norm_gain + norm_bias


def merge_pair(first_part, second_part):
    first_max, first_sum, first_out = first_part
    second_max, second_sum, second_out = second_part
    joint_max = jnp.maximum(first_max, second_max)
    first_scale = jnp.exp(first_max - joint_max)
    second_scale = jnp.exp(second_max - joint_max)
    return (
        joint_max,
        first_sum * first_scale + second_sum * second_scale,
        first_out * first_scale[..., None] + second_out * second_scale[..., None],
    )


def partial_attention(queries, keys_here, values_here, visible):
    scores = jnp.einsum(
        "rthe,rphe->rthp", queries, keys_here, preferred_element_type=jnp.float32
    ) * HDIM ** (-0.5)
    highest = jnp.max(jnp.where(visible, scores, NEG), axis=-1)
    weights = jnp.exp(jnp.where(visible, scores - highest[..., None], NEG)).astype(jnp.bfloat16)
    totals = jnp.sum(weights.astype(jnp.float32), axis=-1)
    blended = jnp.einsum(
        "rthp,rphe->rthe", weights, values_here, preferred_element_type=jnp.float32
    )
    return (highest, totals, blended)


def seq_merge(block_max, block_sum, block_out):
    n_seq = lax.axis_size("seq")
    head_shape = block_out.shape
    lanes = head_shape[-2] * head_shape[-1]
    rows = block_out.size // lanes
    stat_rows = block_max.size // lanes
    out2 = block_out.reshape(rows, lanes)
    top = block_max.reshape(stat_rows, lanes)
    total = block_sum.reshape(stat_rows, lanes)
    width = head_shape[-1]
    step = 1
    while step < n_seq:
        pairs = [(i, i ^ step) for i in range(n_seq)]
        packed = jnp.concatenate([out2, top, total], axis=0)
        other = lax.ppermute(packed, "seq", pairs)
        o_out = other[:rows]
        o_top = other[rows : rows + stat_rows]
        o_total = other[rows + stat_rows :]
        joint = jnp.maximum(top, o_top)
        mine = jnp.exp(top - joint)
        theirs = jnp.exp(o_top - joint)
        total = total * mine + o_total * theirs
        mine_rows = jnp.repeat(mine.reshape(rows, lanes // width), width, axis=1)
        theirs_rows = jnp.repeat(theirs.reshape(rows, lanes // width), width, axis=1)
        out2 = out2 * mine_rows + o_out * theirs_rows
        top = joint
        step *= 2
    return (top.reshape(block_max.shape), total.reshape(block_sum.shape), out2.reshape(head_shape))


def on_device(
    tokens,
    cache_keys,
    cache_values,
    held_states,
    recompute_pos,
    cache_len,
    new_prompt,
    w_qkv,
    qkv_bias,
    w_out,
    out_bias,
    attn_gain,
    attn_shift,
    w_up,
    up_bias,
    w_down,
    down_bias,
    ffn_gain,
    ffn_shift,
):
    local_width = w_qkv.shape[2]
    local_heads = local_width // HDIM
    requests = cache_keys.shape[0]
    block_len = cache_keys.shape[1]
    own_rows = tokens.shape[0]
    steps_count = tokens.shape[1]
    block_rows = lax.all_gather(tokens, "head", axis=0, tiled=True)
    triple = (
        jnp.einsum("rtd,kdc->rtkc", block_rows, w_qkv, preferred_element_type=jnp.float32)
        + qkv_bias
    )
    triple = triple.astype(jnp.bfloat16).reshape(
        block_rows.shape[0], block_rows.shape[1], 3 * local_width
    )
    gathered = jnp.concatenate([triple, block_rows], axis=2)
    head_shape = (requests, steps_count, local_heads, HDIM)
    queries = gathered[:, :, :local_width].reshape(head_shape)
    new_keys = gathered[:, :, local_width : 2 * local_width].reshape(head_shape)
    new_values = gathered[:, :, 2 * local_width : 3 * local_width].reshape(head_shape)
    fresh_keys = (
        jnp.einsum("rjd,dc->rjc", held_states, w_qkv[1], preferred_element_type=jnp.float32)
        + qkv_bias[1]
    ).astype(jnp.bfloat16)
    offset_pos = lax.axis_index("seq") * block_len
    positions = jnp.arange(block_len, dtype=jnp.int32)
    matches = (recompute_pos - offset_pos)[:, :, None] == positions[None, None, :]
    placed = jnp.einsum(
        "rjp,rjc->rpc", matches.astype(jnp.bfloat16), fresh_keys, preferred_element_type=jnp.float32
    ).astype(jnp.bfloat16)
    replaced = jnp.any(matches, axis=1)
    keys_here = jnp.where(replaced[:, :, None], placed, cache_keys).reshape(
        requests, block_len, local_heads, HDIM
    )
    values_here = cache_values.reshape(requests, block_len, local_heads, HDIM)
    visible = ((offset_pos + positions)[None, :] < cache_len[:, None]) & (new_prompt[:, None] == 0)
    block_max, block_sum, block_out = partial_attention(
        queries, keys_here, values_here, visible[:, None, None, :]
    )
    cache_max, cache_sum, cache_out = seq_merge(block_max, block_sum, block_out)
    order_t = jnp.arange(steps_count, dtype=jnp.int32)
    causal = (order_t[:, None] >= order_t[None, :])[None, :, None, :]
    new_max, new_sum, new_out = partial_attention(queries, new_keys, new_values, causal)
    joint_max, joint_sum, joint_out = merge_pair(
        (cache_max, cache_sum, cache_out), (new_max, new_sum, new_out)
    )
    attended = (
        (joint_out / joint_sum[..., None])
        .astype(jnp.bfloat16)
        .reshape(requests, steps_count, local_width)
    )
    head_terms = jnp.einsum("rtc,cd->rtd", attended, w_out, preferred_element_type=jnp.float32)
    summed = lax.psum(head_terms, "head")
    inputs_all = gathered[:, :, 3 * local_width :]
    normed_all = layer_norm(
        inputs_all.astype(jnp.float32) + summed + out_bias, attn_gain, attn_shift
    ).astype(jnp.bfloat16)
    hidden_all = jax.nn.gelu(
        jnp.einsum("rtd,df->rtf", normed_all, w_up, preferred_element_type=jnp.float32) + up_bias,
        approximate=False,
    ).astype(jnp.bfloat16)
    normed = lax.dynamic_slice_in_dim(normed_all, lax.axis_index("head") * own_rows, own_rows, 0)
    reduced = lax.psum_scatter(
        jnp.einsum("rtf,fd->rtd", hidden_all, w_down, preferred_element_type=jnp.float32),
        "head",
        scatter_dimension=0,
        tiled=True,
    )
    return layer_norm(normed.astype(jnp.float32) + reduced + down_bias, ffn_gain, ffn_shift).astype(
        jnp.bfloat16
    )


def solution(mesh):
    placed = (
        P("head", None, None),
        P(None, "seq", "head"),
        P(None, "seq", "head"),
        P(None, "seq", None),
        P(None, "seq"),
        P(),
        P(),
        P(None, None, "head"),
        P(None, "head"),
        P("head", None),
        P(),
        P(),
        P(),
        P(None, "head"),
        P("head"),
        P("head", None),
        P(),
        P(),
        P(),
    )
    return jax.shard_map(
        on_device, mesh=mesh, in_specs=placed, out_specs=P("head", None, None), check_vma=False
    )
```

profile of v0, /device:TPU:8, one launch (start us, length us, event | category | flops | bytes accessed | tf_op | source)
XLA Modules:
  0.0 232.6 jit_solution(7463980318247415298)
XLA Ops:
  6.5 0.8 broadcast_compare_fusion
  7.3 0.7 slice_bitcast_fusion
  8.0 0.7 broadcast_subtract_fusion
  9.0 1.0 copy.122
  10.0 13.1 %all_gather.3 = bf16[64,4,1024]{2,0,1:T(8,128)(2,1)S(1)} all-gather(bf16[16,4,1024]{2,0,1:T(8,128)(2,1)S(1)} %copy.122), channel_id=1, replica_groups=mesh['seq'=128,'head'=4] {'head'}, dimensions={0}, use_global_device_ids=true | all-gather | bytes 655360 | tf_op jit(solution)/shard_map/all_gather | solution.py:101
  23.1 0.4 fusion.7
  23.6 0.7 fusion.131
  24.3 0.8 reshape.249
  25.0 0.3 fusion.8
  25.3 0.7 copy-done.18
  26.1 0.9 fusion
  27.0 0.4 reshape.247
  27.7 1.7 select_reduce_fusion
  29.4 0.5 copy.131
  29.9 0.4 convert_reduce_fusion
  30.4 0.5 copy.132
  31.2 0.4 reshape.250
  31.6 0.4 convolution_bitcast_fusion.1
  32.4 1.9 collective-permute-start
  34.3 1.3 collective-permute-done
  36.4 3.8 %collective-permute-start.1 = (f32[264,128]{1,0:T(8,128)S(1)}, f32[264,128]{1,0:T(8,128)S(1)}, u32[]{:S(2)}, u32[]{:S(2)}) collective-permute-start(f32[264,128]{1,0:T(8,128)S(1)} %pad_maximum_fusion.1), channel_id=1, source_target_pairs={{0,8},{4,12},{8,0},{12,4},{16,24},{20,28},{24,16},{28,20},{32,40},... | collective-permute-start | bytes 405512 | tf_op jit(solution)/shard_map/ppermute | solution.py:58
  40.3 3.9 %collective-permute-done.1 = f32[264,128]{1,0:T(8,128)S(1)} collective-permute-done((f32[264,128]{1,0:T(8,128)S(1)}, f32[264,128]{1,0:T(8,128)S(1)}, u32[]{:S(2)}, u32[]{:S(2)}) %collective-permute-start.1) | collective-permute-done | bytes 135200 | tf_op jit(solution)/shard_map/ppermute | solution.py:58
  44.9 5.2 %collective-permute-start.2 = (f32[264,128]{1,0:T(8,128)S(1)}, f32[264,128]{1,0:T(8,128)S(1)}, u32[]{:S(2)}, u32[]{:S(2)}) collective-permute-start(f32[264,128]{1,0:T(8,128)S(1)} %pad_maximum_fusion.2), channel_id=1, source_target_pairs={{0,16},{4,20},{8,24},{12,28},{16,0},{20,4},{24,8},{28,12},{32,48},... | collective-permute-start | bytes 405512 | tf_op jit(solution)/shard_map/ppermute | solution.py:58
  50.1 6.1 %collective-permute-done.2 = f32[264,128]{1,0:T(8,128)S(1)} collective-permute-done((f32[264,128]{1,0:T(8,128)S(1)}, f32[264,128]{1,0:T(8,128)S(1)}, u32[]{:S(2)}, u32[]{:S(2)}) %collective-permute-start.2) | collective-permute-done | bytes 135200 | tf_op jit(solution)/shard_map/ppermute | solution.py:58
  57.0 9.1 %collective-permute-start.3 = (f32[264,128]{1,0:T(8,128)S(1)}, f32[264,128]{1,0:T(8,128)S(1)}, u32[]{:S(2)}, u32[]{:S(2)}) collective-permute-start(f32[264,128]{1,0:T(8,128)S(1)} %pad_maximum_fusion.3), channel_id=1, source_target_pairs={{0,32},{4,36},{8,40},{12,44},{16,48},{20,52},{24,56},{28,60},{32,0... | collective-permute-start | bytes 405512 | tf_op jit(solution)/shard_map/ppermute | solution.py:58
  66.2 10.2 %collective-permute-done.3 = f32[264,128]{1,0:T(8,128)S(1)} collective-permute-done((f32[264,128]{1,0:T(8,128)S(1)}, f32[264,128]{1,0:T(8,128)S(1)}, u32[]{:S(2)}, u32[]{:S(2)}) %collective-permute-start.3) | collective-permute-done | bytes 135200 | tf_op jit(solution)/shard_map/ppermute | solution.py:58
  77.1 13.6 %collective-permute-start.4 = (f32[264,128]{1,0:T(8,128)S(1)}, f32[264,128]{1,0:T(8,128)S(1)}, u32[]{:S(2)}, u32[]{:S(2)}) collective-permute-start(f32[264,128]{1,0:T(8,128)S(1)} %pad_maximum_fusion.4), channel_id=1, source_target_pairs={{0,64},{4,68},{8,72},{12,76},{16,80},{20,84},{24,88},{28,92},{32,9... | collective-permute-start | bytes 405512 | tf_op jit(solution)/shard_map/ppermute | solution.py:58
  91.0 12.1 %collective-permute-done.4 = f32[264,128]{1,0:T(8,128)S(1)} collective-permute-done((f32[264,128]{1,0:T(8,128)S(1)}, f32[264,128]{1,0:T(8,128)S(1)}, u32[]{:S(2)}, u32[]{:S(2)}) %collective-permute-start.4) | collective-permute-done | bytes 135200 | tf_op jit(solution)/shard_map/ppermute | solution.py:58
  103.9 3.5 %collective-permute-start.5 = (f32[264,128]{1,0:T(8,128)S(1)}, f32[264,128]{1,0:T(8,128)S(1)}, u32[]{:S(2)}, u32[]{:S(2)}) collective-permute-start(f32[264,128]{1,0:T(8,128)S(1)} %pad_maximum_fusion.5), channel_id=1, source_target_pairs={{0,128},{4,132},{8,136},{12,140},{16,144},{20,148},{24,152},{28,15... | collective-permute-start | bytes 405512 | tf_op jit(solution)/shard_map/ppermute | solution.py:58
  107.8 3.3 %collective-permute-done.5 = f32[264,128]{1,0:T(8,128)S(1)} collective-permute-done((f32[264,128]{1,0:T(8,128)S(1)}, f32[264,128]{1,0:T(8,128)S(1)}, u32[]{:S(2)}, u32[]{:S(2)}) %collective-permute-start.5) | collective-permute-done | bytes 135200 | tf_op jit(solution)/shard_map/ppermute | solution.py:58
  111.9 3.9 %collective-permute-start.6 = (f32[264,128]{1,0:T(8,128)S(1)}, f32[264,128]{1,0:T(8,128)S(1)}, u32[]{:S(2)}, u32[]{:S(2)}) collective-permute-start(f32[264,128]{1,0:T(8,128)S(1)} %pad_maximum_fusion.6), channel_id=1, source_target_pairs={{0,256},{4,260},{8,264},{12,268},{16,272},{20,276},{24,280},{28,28... | collective-permute-start | bytes 405512 | tf_op jit(solution)/shard_map/ppermute | solution.py:58
  116.1 4.2 %collective-permute-done.6 = f32[264,128]{1,0:T(8,128)S(1)} collective-permute-done((f32[264,128]{1,0:T(8,128)S(1)}, f32[264,128]{1,0:T(8,128)S(1)}, u32[]{:S(2)}, u32[]{:S(2)}) %collective-permute-start.6) | collective-permute-done | bytes 135200 | tf_op jit(solution)/shard_map/ppermute | solution.py:58
  122.3 0.5 fusion.6
  123.0 0.7 copy-done.6
  123.7 1.3 fusion.29
  125.3 58.1 %all-reduce.2.cloned.1.call-done = f32[64,4,1024]{2,0,1:T(8,128)} async-done(((f32[64,4,1024]{2,0,1:T(8,128)}), f32[64,4,1024]{2,0,1:T(8,128)}) %all-reduce.2.cloned.1.call-update) | async-done | bytes 1048592 | tf_op jit(solution)/shard_map/psum | solution.py:146
  183.4 1.5 fusion.26
  185.0 0.3 multiply_reduce_fusion
  185.3 0.4 copy-done.11
  185.7 0.3 copy-done.10
  186.0 0.3 add_convert_fusion
  186.3 0.9 copy-done.16
  187.2 0.6 fusion.75
  187.8 2.5 %fusion.9 = f32[64,4,1024]{2,0,1:T(8,128)} fusion(bf16[512,1024]{1,0:T(8,128)(2,1)S(1)} %copy-done, f32[64,4,512]{2,0,1:T(8,128)S(1)} %get-tuple-element.45, u8[64,512]{1,0:T(8,128)(4,1)S(1)} %get-tuple-element.6, u8[64,512]{1,0:T(8,128)(4,1)S(1)} %get-tuple-element.5), kind=kOutput, calls=%fused_computation.16 | convolution fusion | flops 277610496 | bytes 2686976 | tf_op jit(solution)/shard_map/rtf,fd->rtd/dot_general | solution.py:157
  190.3 32.6 %reduce-scatter.2.cloned.1.call-done = f32[16,4,1024]{2,0,1:T(8,128)} async-done(((f32[64,4,1024]{2,0,1:T(8,128)}), f32[16,4,1024]{2,0,1:T(8,128)}) %reduce-scatter.2.cloned.1.call-update) | async-done | bytes 262160 | tf_op jit(solution)/shard_map/reduce_scatter | solution.py:156
  222.9 1.1 fusion.82
  224.2 0.7 copy-done.12
  225.0 0.8 copy.180
  (149 shorter events, 9.3 us)
Async XLA Ops:
  6.5 181.2 %copy-start = (bf16[512,1024]{1,0:T(8,128)(2,1)S(1)}, bf16[512,1024]{1,0:T(8,128)(2,1)}, u32[]{:S(2)}) copy-start(bf16[512,1024]{1,0:T(8,128)(2,1)} %param.34) | copy-start | bytes 3145732
  6.5 16.6 %copy-start.3 = (bf16[3,1024,128]{2,1,0:T(8,128)(2,1)S(1)}, bf16[3,1024,128]{2,1,0:T(8,128)(2,1)}, u32[]{:S(2)}) copy-start(bf16[3,1024,128]{2,1,0:T(8,128)(2,1)} %param.26) | copy-start | bytes 2359300
  6.5 176.9 %all-reduce.2.cloned.1.call-start = ((), (), s32[]{:S(2)}) async-start(), calls=%async_computation.1 | async-start | bytes 2097152 | tf_op jit(solution)/shard_map/psum | solution.py:146
  9.9 13.2 %copy-start.14 = (f32[3,128]{1,0:T(4,128)S(1)}, f32[3,128]{1,0:T(4,128)}, u32[]{:S(2)}) copy-start(f32[3,128]{1,0:T(4,128)} %param.27) | copy-start | bytes 4612
  23.5 1.5 copy-start.17
  25.0 1.0 copy-start.18
  27.0 0.7 copy-start.15
  29.4 1.8 copy-start.4
  32.4 3.2 %collective-permute-start = (f32[264,128]{1,0:T(8,128)S(1)}, f32[264,128]{1,0:T(8,128)S(1)}, u32[]{:S(2)}, u32[]{:S(2)}) collective-permute-start(f32[264,128]{1,0:T(8,128)S(1)} %pad_maximum_fusion), channel_id=1, source_target_pairs={{0,4},{4,0},{8,12},{12,8},{16,20},{20,16},{24,28},{28,24},{32,36},... | collective-permute-start | bytes 405512 | tf_op jit(solution)/shard_map/ppermute | solution.py:58
  36.4 7.7 %collective-permute-start.1 = (f32[264,128]{1,0:T(8,128)S(1)}, f32[264,128]{1,0:T(8,128)S(1)}, u32[]{:S(2)}, u32[]{:S(2)}) collective-permute-start(f32[264,128]{1,0:T(8,128)S(1)} %pad_maximum_fusion.1), channel_id=1, source_target_pairs={{0,8},{4,12},{8,0},{12,4},{16,24},{20,28},{24,16},{28,20},{32,40},... | collective-permute-start | bytes 405512 | tf_op jit(solution)/shard_map/ppermute | solution.py:58
  44.9 11.3 %collective-permute-start.2 = (f32[264,128]{1,0:T(8,128)S(1)}, f32[264,128]{1,0:T(8,128)S(1)}, u32[]{:S(2)}, u32[]{:S(2)}) collective-permute-start(f32[264,128]{1,0:T(8,128)S(1)} %pad_maximum_fusion.2), channel_id=1, source_target_pairs={{0,16},{4,20},{8,24},{12,28},{16,0},{20,4},{24,8},{28,12},{32,48},... | collective-permute-start | bytes 405512 | tf_op jit(solution)/shard_map/ppermute | solution.py:58
  56.9 9.1 %copy-start.5 = (bf16[64,4,128]{2,0,1:T(8,128)(2,1)S(1)}, bf16[64,4,128]{2,0,1:T(8,128)(2,1)}, u32[]{:S(2)}) copy-start(bf16[64,4,128]{2,0,1:T(8,128)(2,1)} %get-tuple-element.41) | copy-start | bytes 196612
  57.0 19.4 %collective-permute-start.3 = (f32[264,128]{1,0:T(8,128)S(1)}, f32[264,128]{1,0:T(8,128)S(1)}, u32[]{:S(2)}, u32[]{:S(2)}) collective-permute-start(f32[264,128]{1,0:T(8,128)S(1)} %pad_maximum_fusion.3), channel_id=1, source_target_pairs={{0,32},{4,36},{8,40},{12,44},{16,48},{20,52},{24,56},{28,60},{32,0... | collective-permute-start | bytes 405512 | tf_op jit(solution)/shard_map/ppermute | solution.py:58
  77.1 13.6 %copy-start.7 = (bf16[64,4,2,64]{3,2,0,1:T(2,128)(2,1)S(1)}, bf16[64,4,2,64]{3,2,0,1:T(2,128)(2,1)}, u32[]{:S(2)}) copy-start(bf16[64,4,2,64]{3,2,0,1:T(2,128)(2,1)} %reshape.249) | copy-start | bytes 196612
  77.1 26.0 %collective-permute-start.4 = (f32[264,128]{1,0:T(8,128)S(1)}, f32[264,128]{1,0:T(8,128)S(1)}, u32[]{:S(2)}, u32[]{:S(2)}) collective-permute-start(f32[264,128]{1,0:T(8,128)S(1)} %pad_maximum_fusion.4), channel_id=1, source_target_pairs={{0,64},{4,68},{8,72},{12,76},{16,80},{20,84},{24,88},{28,92},{32,9... | collective-permute-start | bytes 405512 | tf_op jit(solution)/shard_map/ppermute | solution.py:58
  103.9 7.2 %collective-permute-start.5 = (f32[264,128]{1,0:T(8,128)S(1)}, f32[264,128]{1,0:T(8,128)S(1)}, u32[]{:S(2)}, u32[]{:S(2)}) collective-permute-start(f32[264,128]{1,0:T(8,128)S(1)} %pad_maximum_fusion.5), channel_id=1, source_target_pairs={{0,128},{4,132},{8,136},{12,140},{16,144},{20,148},{24,152},{28,15... | collective-permute-start | bytes 405512 | tf_op jit(solution)/shard_map/ppermute | solution.py:58
  111.9 8.4 %collective-permute-start.6 = (f32[264,128]{1,0:T(8,128)S(1)}, f32[264,128]{1,0:T(8,128)S(1)}, u32[]{:S(2)}, u32[]{:S(2)}) collective-permute-start(f32[264,128]{1,0:T(8,128)S(1)} %pad_maximum_fusion.6), channel_id=1, source_target_pairs={{0,256},{4,260},{8,264},{12,268},{16,272},{20,276},{24,280},{28,28... | collective-permute-start | bytes 405512 | tf_op jit(solution)/shard_map/ppermute | solution.py:58
  122.8 1.0 copy-start.6
  125.1 58.4 %copy-start.8 = (f32[1024]{0:T(1024)S(1)}, f32[1024]{0:T(1024)}, u32[]{:S(2)}) copy-start(f32[1024]{0:T(1024)} %param.29) | copy-start | bytes 12292
  125.1 97.8 %reduce-scatter.2.cloned.1.call-start = ((), (), s32[]{:S(2)}) async-start(), calls=%async_computation.2 | async-start | bytes 1310720 | tf_op jit(solution)/shard_map/reduce_scatter | solution.py:156
  183.4 1.5 copy-start.1
  185.0 0.7 copy-start.11
  185.3 0.7 copy-start.10
  186.0 1.2 copy-start.16
  186.0 1.2 copy-start.19
  190.3 32.6 %copy-start.9 = (f32[1024]{0:T(1024)S(1)}, f32[1024]{0:T(1024)}, u32[]{:S(2)}) copy-start(f32[1024]{0:T(1024)} %param.35) | copy-start | bytes 12292
  222.9 1.1 copy-start.2
  222.9 1.4 copy-start.13
  224.2 0.7 copy-start.12
Sparse Core Ops, SparseCore 0:
  125.2 58.1 all-reduce.1
  190.4 32.4 reduce-scatter.1
where the time goes:
time: 233 us
  waiting for transfers between devices  132 us (57%)
  starting transfers between devices  41.2 us (18%)
  local copies, waits for them, and re-layouts  16.8 us (7%)
  between operations  14.3 us (6%)
  blocking collectives  13.1 us (6%)
  matrix products  8.92 us (4%)
  other arithmetic  6.39 us (3%)
    psum x1, waiting for transfers between devices, on_device(): summed = lax.psum(head_terms, 'head')  58.1 us
    ppermute x7, waiting for transfers between devices, seq_merge(): other = lax.ppermute(packed, 'seq', pairs)  41.2 us
    ppermute x7, starting transfers between devices, seq_merge(): other = lax.ppermute(packed, 'seq', pairs)  41 us
    reduce_scatter x1, waiting for transfers between devices, on_device(): lax.psum_scatter(jnp.einsum('rtf,fd->rtd', hidden_all, w_down, preferred_...  32.6 us
    all_gather x1, blocking collectives, on_device(): block_rows = lax.all_gather(tokens, 'head', axis=0, tiled=True)  13.1 us
    unnamed x41, local copies, waits for them, and re-layouts  4.99 us
  transfers between devices with their start and end apart: 9, of which 9 were waited for; matrix products, arithmetic and copies ran while one was open for 0% of the time, Pallas kernels for 0%

commit v1 on v0

--- a/solution.py
+++ b/solution.py
@@ -98,7 +98,9 @@
     block_len = cache_keys.shape[1]
     own_rows = tokens.shape[0]
     steps_count = tokens.shape[1]
-    block_rows = lax.all_gather(tokens, "head", axis=0, tiled=True)
+    block_rows = jnp.concatenate(
+        lax.all_to_all(jnp.stack([tokens] * lax.axis_size("head")), "head", 0, 0), axis=0
+    )
     triple = (
         jnp.einsum("rtd,kdc->rtkc", block_rows, w_qkv, preferred_element_type=jnp.float32)
         + qkv_bias

time: 233 us -> 228 us (0.979)
  blocking collectives: 13.1 us -> 0 us
  starting transfers between devices: 41.2 us -> 45.3 us
  matrix products: 8.92 us -> 11.4 us
    all_gather x1 -> x0, blocking collectives: 13.1 us -> none  [on_device(): block_rows = lax.all_gather(tokens, 'head', axis=0, tiled=True)]
    all_to_all x0 -> x1, starting transfers between devices: none -> 4.42 us  [on_device(): lax.all_to_all(jnp.stack([tokens] * lax.axis_size('head')), 'head', 0, 0)]
    all_to_all x0 -> x1, waiting for transfers between devices: none -> 2.73 us  [on_device(): lax.all_to_all(jnp.stack([tokens] * lax.axis_size('head')), 'head', 0, 0)]
    unnamed x41 -> x39, local copies, waits for them, and re-layouts: 4.99 us -> 6.32 us
  transfers between devices with their start and end apart: 9 -> 10, of which waited for: 9 -> 10; matrix products, arithmetic and copies ran while one was open for 0% -> 2% of each run, Pallas kernels for 0% -> 0%
where the time goes in v1:
time: 228 us; the launch traced here: 227 us
  waiting for transfers between devices  133 us (58%)
  starting transfers between devices  45.3 us (20%)
  local copies, waits for them, and re-layouts  18.1 us (8%)
  between operations  14.2 us (6%)
  matrix products  11.4 us (5%)
  other arithmetic  4.88 us (2%)
    psum x1, waiting for transfers between devices, on_device(): summed = lax.psum(head_terms, 'head')  56.7 us
    ppermute x7, waiting for transfers between devices, seq_merge(): other = lax.ppermute(packed, 'seq', pairs)  41.1 us
    ppermute x7, starting transfers between devices, seq_merge(): other = lax.ppermute(packed, 'seq', pairs)  40.6 us
    reduce_scatter x1, waiting for transfers between devices, on_device(): lax.psum_scatter(jnp.einsum('rtf,fd->rtd', hidden_all, w_down, preferred_...  32.6 us
    unnamed x39, local copies, waits for them, and re-layouts  6.32 us
  transfers between devices with their start and end apart: 10, of which 10 were waited for; matrix products, arithmetic and copies ran while one was open for 2% of the time, Pallas kernels for 0%

profile of v1, /device:TPU:8, one launch (start us, length us, event | category | flops | bytes accessed | tf_op | source)
XLA Modules:
  0.0 227.0 jit_solution(13343844990313190711)
XLA Ops:
  6.5 1.0 copy.123
  7.6 0.9 stack.2
  8.5 4.4 %all-to-all-start = ((bf16[4,16,4,1024]{3,1,2,0:T(8,128)(2,1)}), bf16[4,16,4,1024]{3,1,2,0:T(8,128)(2,1)S(1)}, u32[]{:S(2)}, u32[]{:S(2)}) async-start(bf16[4,16,4,1024]{3,1,2,0:T(8,128)(2,1)} %stack.2), calls=%async_computation | async-start | bytes 1048576 | tf_op jit(solution)/shard_map/all_to_all | solution.py:102
  12.9 0.7 copy-done.11
  13.6 0.7 copy-done.12
  14.6 1.3 fusion.8
  15.9 0.9 fusion
  16.8 1.4 reshape.253
  18.2 0.4 reshape.256
  18.9 0.6 copy-done.13
  19.6 2.7 %all-to-all-done = bf16[4,16,4,1024]{3,1,2,0:T(8,128)(2,1)S(1)} async-done(((bf16[4,16,4,1024]{3,1,2,0:T(8,128)(2,1)}), bf16[4,16,4,1024]{3,1,2,0:T(8,128)(2,1)S(1)}, u32[]{:S(2)}, u32[]{:S(2)}) %all-to-all-start) | async-done | bytes 524320 | tf_op jit(solution)/shard_map/all_to_all | solution.py:102
  22.4 1.6 fusion.7
  24.2 2.0 select_reduce_fusion
  26.2 0.5 copy.133
  26.7 0.4 convert_reduce_fusion
  27.1 0.5 copy.134
  27.9 0.5 convolution_bitcast_fusion.1
  28.7 1.9 collective-permute-start
  30.7 1.3 collective-permute-done
  32.7 3.8 %collective-permute-start.1 = (f32[264,128]{1,0:T(8,128)S(1)}, f32[264,128]{1,0:T(8,128)S(1)}, u32[]{:S(2)}, u32[]{:S(2)}) collective-permute-start(f32[264,128]{1,0:T(8,128)S(1)} %pad_maximum_fusion.1), channel_id=1, source_target_pairs={{0,8},{4,12},{8,0},{12,4},{16,24},{20,28},{24,16},{28,20},{32,40},... | collective-permute-start | bytes 405512 | tf_op jit(solution)/shard_map/ppermute | solution.py:58
  36.6 3.9 %collective-permute-done.1 = f32[264,128]{1,0:T(8,128)S(1)} collective-permute-done((f32[264,128]{1,0:T(8,128)S(1)}, f32[264,128]{1,0:T(8,128)S(1)}, u32[]{:S(2)}, u32[]{:S(2)}) %collective-permute-start.1) | collective-permute-done | bytes 135200 | tf_op jit(solution)/shard_map/ppermute | solution.py:58
  41.2 5.2 %collective-permute-start.2 = (f32[264,128]{1,0:T(8,128)S(1)}, f32[264,128]{1,0:T(8,128)S(1)}, u32[]{:S(2)}, u32[]{:S(2)}) collective-permute-start(f32[264,128]{1,0:T(8,128)S(1)} %pad_maximum_fusion.2), channel_id=1, source_target_pairs={{0,16},{4,20},{8,24},{12,28},{16,0},{20,4},{24,8},{28,12},{32,48},... | collective-permute-start | bytes 405512 | tf_op jit(solution)/shard_map/ppermute | solution.py:58
  46.4 6.1 %collective-permute-done.2 = f32[264,128]{1,0:T(8,128)S(1)} collective-permute-done((f32[264,128]{1,0:T(8,128)S(1)}, f32[264,128]{1,0:T(8,128)S(1)}, u32[]{:S(2)}, u32[]{:S(2)}) %collective-permute-start.2) | collective-permute-done | bytes 135200 | tf_op jit(solution)/shard_map/ppermute | solution.py:58
  53.3 9.1 %collective-permute-start.3 = (f32[264,128]{1,0:T(8,128)S(1)}, f32[264,128]{1,0:T(8,128)S(1)}, u32[]{:S(2)}, u32[]{:S(2)}) collective-permute-start(f32[264,128]{1,0:T(8,128)S(1)} %pad_maximum_fusion.3), channel_id=1, source_target_pairs={{0,32},{4,36},{8,40},{12,44},{16,48},{20,52},{24,56},{28,60},{32,0... | collective-permute-start | bytes 405512 | tf_op jit(solution)/shard_map/ppermute | solution.py:58
  62.4 10.3 %collective-permute-done.3 = f32[264,128]{1,0:T(8,128)S(1)} collective-permute-done((f32[264,128]{1,0:T(8,128)S(1)}, f32[264,128]{1,0:T(8,128)S(1)}, u32[]{:S(2)}, u32[]{:S(2)}) %collective-permute-start.3) | collective-permute-done | bytes 135200 | tf_op jit(solution)/shard_map/ppermute | solution.py:58
  73.4 13.4 %collective-permute-start.4 = (f32[264,128]{1,0:T(8,128)S(1)}, f32[264,128]{1,0:T(8,128)S(1)}, u32[]{:S(2)}, u32[]{:S(2)}) collective-permute-start(f32[264,128]{1,0:T(8,128)S(1)} %pad_maximum_fusion.4), channel_id=1, source_target_pairs={{0,64},{4,68},{8,72},{12,76},{16,80},{20,84},{24,88},{28,92},{32,9... | collective-permute-start | bytes 405512 | tf_op jit(solution)/shard_map/ppermute | solution.py:58
  87.0 12.3 %collective-permute-done.4 = f32[264,128]{1,0:T(8,128)S(1)} collective-permute-done((f32[264,128]{1,0:T(8,128)S(1)}, f32[264,128]{1,0:T(8,128)S(1)}, u32[]{:S(2)}, u32[]{:S(2)}) %collective-permute-start.4) | collective-permute-done | bytes 135200 | tf_op jit(solution)/shard_map/ppermute | solution.py:58
  100.1 3.0 %collective-permute-start.5 = (f32[264,128]{1,0:T(8,128)S(1)}, f32[264,128]{1,0:T(8,128)S(1)}, u32[]{:S(2)}, u32[]{:S(2)}) collective-permute-start(f32[264,128]{1,0:T(8,128)S(1)} %pad_maximum_fusion.5), channel_id=1, source_target_pairs={{0,128},{4,132},{8,136},{12,140},{16,144},{20,148},{24,152},{28,15... | collective-permute-start | bytes 405512 | tf_op jit(solution)/shard_map/ppermute | solution.py:58
  103.0 0.3 fusion.70
  103.7 3.3 %collective-permute-done.5 = f32[264,128]{1,0:T(8,128)S(1)} collective-permute-done((f32[264,128]{1,0:T(8,128)S(1)}, f32[264,128]{1,0:T(8,128)S(1)}, u32[]{:S(2)}, u32[]{:S(2)}) %collective-permute-start.5) | collective-permute-done | bytes 135200 | tf_op jit(solution)/shard_map/ppermute | solution.py:58
  107.7 4.2 %collective-permute-start.6 = (f32[264,128]{1,0:T(8,128)S(1)}, f32[264,128]{1,0:T(8,128)S(1)}, u32[]{:S(2)}, u32[]{:S(2)}) collective-permute-start(f32[264,128]{1,0:T(8,128)S(1)} %pad_maximum_fusion.6), channel_id=1, source_target_pairs={{0,256},{4,260},{8,264},{12,268},{16,272},{20,276},{24,280},{28,28... | collective-permute-start | bytes 405512 | tf_op jit(solution)/shard_map/ppermute | solution.py:58
  112.2 3.9 %collective-permute-done.6 = f32[264,128]{1,0:T(8,128)S(1)} collective-permute-done((f32[264,128]{1,0:T(8,128)S(1)}, f32[264,128]{1,0:T(8,128)S(1)}, u32[]{:S(2)}, u32[]{:S(2)}) %collective-permute-start.6) | collective-permute-done | bytes 135200 | tf_op jit(solution)/shard_map/ppermute | solution.py:58
  118.1 0.5 fusion.6
  118.9 0.7 copy-done.4
  119.6 1.3 fusion.28
  121.1 56.7 %all-reduce.2.cloned.1.call-done = f32[64,4,1024]{2,0,1:T(8,128)} async-done(((f32[64,4,1024]{2,0,1:T(8,128)}), f32[64,4,1024]{2,0,1:T(8,128)}) %all-reduce.2.cloned.1.call-update) | async-done | bytes 1048592 | tf_op jit(solution)/shard_map/psum | solution.py:148
  177.8 1.5 fusion.25
  179.4 0.3 multiply_reduce_fusion
  179.7 0.4 copy-done.8
  180.1 0.3 copy-done.7
  180.4 0.3 add_convert_fusion
  180.7 0.9 copy-done.14
  181.6 0.6 fusion.74
  182.2 2.5 %fusion.9 = f32[64,4,1024]{2,0,1:T(8,128)} fusion(bf16[512,1024]{1,0:T(8,128)(2,1)S(1)} %copy-done, f32[64,4,512]{2,0,1:T(8,128)S(1)} %get-tuple-element.45, u8[64,512]{1,0:T(8,128)(4,1)S(1)} %get-tuple-element.6, u8[64,512]{1,0:T(8,128)(4,1)S(1)} %get-tuple-element.5), kind=kOutput, calls=%fused_computation.16 | convolution fusion | flops 277610496 | bytes 2686976 | tf_op jit(solution)/shard_map/rtf,fd->rtd/dot_general | solution.py:159
  184.7 32.6 %reduce-scatter.2.cloned.1.call-done = f32[16,4,1024]{2,0,1:T(8,128)} async-done(((f32[64,4,1024]{2,0,1:T(8,128)}), f32[16,4,1024]{2,0,1:T(8,128)}) %reduce-scatter.2.cloned.1.call-update) | async-done | bytes 262160 | tf_op jit(solution)/shard_map/reduce_scatter | solution.py:158
  217.3 1.1 fusion.81
  218.7 0.7 copy-done.9
  219.4 0.8 copy.182
  (150 shorter events, 9.1 us)
Async XLA Ops:
  6.5 175.6 %copy-start = (bf16[512,1024]{1,0:T(8,128)(2,1)S(1)}, bf16[512,1024]{1,0:T(8,128)(2,1)}, u32[]{:S(2)}) copy-start(bf16[512,1024]{1,0:T(8,128)(2,1)} %param.34) | copy-start | bytes 3145732
  8.4 6.1 %copy-start.15 = (bf16[64,4,1024]{2,1,0:T(4,128)(2,1)S(1)}, bf16[64,4,1024]{2,1,0:T(4,128)(2,1)}, u32[]{:S(2)}) copy-start(bf16[64,4,1024]{2,1,0:T(4,128)(2,1)} %param.22) | copy-start | bytes 1572868
  8.5 13.9 %all-to-all-start = ((bf16[4,16,4,1024]{3,1,2,0:T(8,128)(2,1)}), bf16[4,16,4,1024]{3,1,2,0:T(8,128)(2,1)S(1)}, u32[]{:S(2)}, u32[]{:S(2)}) async-start(bf16[4,16,4,1024]{3,1,2,0:T(8,128)(2,1)} %stack.2), calls=%async_computation | async-start | bytes 1048576 | tf_op jit(solution)/shard_map/all_to_all | solution.py:102
  12.9 164.9 %all-reduce.2.cloned.1.call-start = ((), (), s32[]{:S(2)}) async-start(), calls=%async_computation.2 | async-start | bytes 2097152 | tf_op jit(solution)/shard_map/psum | solution.py:148
  12.9 0.7 copy-start.11
  13.6 0.7 copy-start.12
  14.5 1.3 copy-start.16
  16.8 1.4 copy-start.3
  18.2 0.7 copy-start.18
  18.9 0.7 copy-start.13
  28.7 3.2 %collective-permute-start = (f32[264,128]{1,0:T(8,128)S(1)}, f32[264,128]{1,0:T(8,128)S(1)}, u32[]{:S(2)}, u32[]{:S(2)}) collective-permute-start(f32[264,128]{1,0:T(8,128)S(1)} %pad_maximum_fusion), channel_id=1, source_target_pairs={{0,4},{4,0},{8,12},{12,8},{16,20},{20,16},{24,28},{28,24},{32,36},... | collective-permute-start | bytes 405512 | tf_op jit(solution)/shard_map/ppermute | solution.py:58
  32.7 7.7 %collective-permute-start.1 = (f32[264,128]{1,0:T(8,128)S(1)}, f32[264,128]{1,0:T(8,128)S(1)}, u32[]{:S(2)}, u32[]{:S(2)}) collective-permute-start(f32[264,128]{1,0:T(8,128)S(1)} %pad_maximum_fusion.1), channel_id=1, source_target_pairs={{0,8},{4,12},{8,0},{12,4},{16,24},{20,28},{24,16},{28,20},{32,40},... | collective-permute-start | bytes 405512 | tf_op jit(solution)/shard_map/ppermute | solution.py:58
  41.2 11.3 %collective-permute-start.2 = (f32[264,128]{1,0:T(8,128)S(1)}, f32[264,128]{1,0:T(8,128)S(1)}, u32[]{:S(2)}, u32[]{:S(2)}) collective-permute-start(f32[264,128]{1,0:T(8,128)S(1)} %pad_maximum_fusion.2), channel_id=1, source_target_pairs={{0,16},{4,20},{8,24},{12,28},{16,0},{20,4},{24,8},{28,12},{32,48},... | collective-permute-start | bytes 405512 | tf_op jit(solution)/shard_map/ppermute | solution.py:58
  53.3 19.4 %collective-permute-start.3 = (f32[264,128]{1,0:T(8,128)S(1)}, f32[264,128]{1,0:T(8,128)S(1)}, u32[]{:S(2)}, u32[]{:S(2)}) collective-permute-start(f32[264,128]{1,0:T(8,128)S(1)} %pad_maximum_fusion.3), channel_id=1, source_target_pairs={{0,32},{4,36},{8,40},{12,44},{16,48},{20,52},{24,56},{28,60},{32,0... | collective-permute-start | bytes 405512 | tf_op jit(solution)/shard_map/ppermute | solution.py:58
  73.4 25.9 %collective-permute-start.4 = (f32[264,128]{1,0:T(8,128)S(1)}, f32[264,128]{1,0:T(8,128)S(1)}, u32[]{:S(2)}, u32[]{:S(2)}) collective-permute-start(f32[264,128]{1,0:T(8,128)S(1)} %pad_maximum_fusion.4), channel_id=1, source_target_pairs={{0,64},{4,68},{8,72},{12,76},{16,80},{20,84},{24,88},{28,92},{32,9... | collective-permute-start | bytes 405512 | tf_op jit(solution)/shard_map/ppermute | solution.py:58
  100.1 6.9 %collective-permute-start.5 = (f32[264,128]{1,0:T(8,128)S(1)}, f32[264,128]{1,0:T(8,128)S(1)}, u32[]{:S(2)}, u32[]{:S(2)}) collective-permute-start(f32[264,128]{1,0:T(8,128)S(1)} %pad_maximum_fusion.5), channel_id=1, source_target_pairs={{0,128},{4,132},{8,136},{12,140},{16,144},{20,148},{24,152},{28,15... | collective-permute-start | bytes 405512 | tf_op jit(solution)/shard_map/ppermute | solution.py:58
  107.7 8.4 %collective-permute-start.6 = (f32[264,128]{1,0:T(8,128)S(1)}, f32[264,128]{1,0:T(8,128)S(1)}, u32[]{:S(2)}, u32[]{:S(2)}) collective-permute-start(f32[264,128]{1,0:T(8,128)S(1)} %pad_maximum_fusion.6), channel_id=1, source_target_pairs={{0,256},{4,260},{8,264},{12,268},{16,272},{20,276},{24,280},{28,28... | collective-permute-start | bytes 405512 | tf_op jit(solution)/shard_map/ppermute | solution.py:58
  118.6 1.0 copy-start.4
  120.9 56.9 %copy-start.5 = (f32[1024]{0:T(1024)S(1)}, f32[1024]{0:T(1024)}, u32[]{:S(2)}) copy-start(f32[1024]{0:T(1024)} %param.29) | copy-start | bytes 12292
  120.9 96.4 %reduce-scatter.2.cloned.1.call-start = ((), (), s32[]{:S(2)}) async-start(), calls=%async_computation.3 | async-start | bytes 1310720 | tf_op jit(solution)/shard_map/reduce_scatter | solution.py:158
  177.8 1.5 copy-start.1
  179.4 0.7 copy-start.8
  179.7 0.7 copy-start.7
  180.4 1.2 copy-start.14
  180.4 1.2 copy-start.17
  184.7 32.6 %copy-start.6 = (f32[1024]{0:T(1024)S(1)}, f32[1024]{0:T(1024)}, u32[]{:S(2)}) copy-start(f32[1024]{0:T(1024)} %param.35) | copy-start | bytes 12292
  217.3 1.1 copy-start.2
  217.3 1.4 copy-start.10
  218.6 0.7 copy-start.9
Sparse Core Ops, SparseCore 0:
  121.0 56.7 all-reduce.1
  184.8 32.4 reduce-scatter.1
